TPU v7x, 256 devices: a whole 4x4x8 slice. The times are simulated.
256 devices in a mesh: row: 8 (over y, x_lo), col: 32 (over x_hi, z, core).
Axes of the slice: x: 4 (x_hi: 2, x_lo: 2; x = x_hi * 2 + x_lo), y: 4, z: 8, core: 2. Of those that a mesh axis runs over, the one named last changes fastest.
Arguments:
- vectors: bfloat16 [16, 131072], P(None, ('row', 'col')), may hold values from -6 to 6
- blocks: bfloat16 [8, 6144, 128, 128], P('row', 'col'), may hold values from -0.09375 to 0.09375
- row_ptr: int32 [8, 4128], P('row', 'col'), may hold values from 0 to 192, as said below
- col_idx: int32 [8, 6144], P('row', 'col'), may hold values from 0 to 31, as said below
Outputs:
- product: float32 [16, 131072], P(None, ('row', 'col'))
Inputs may be any that keep to these rules, and one draw needn't show every extreme that they name: For each tile, row_ptr starts at 0, never falls, and ends at the tile's count of live slots; at least one tile has exactly 192 live slots in every draw, and counts differ strongly from tile to tile. `col_idx`: within each block row of a tile the live slots name strictly rising block columns, so no block position of a tile is stored twice; slots at or past a tile's count hold a valid column and are unused.
All inputs are finite; a program needn't handle non-finite values.
Results may differ from a plain program's by a relative error of at most 0.0003.
Values may be sent and summed in bfloat16 or wider, within the bound.
No kernel may reach another device: no remote copies, remote signals or barrier semaphores. Data moves between devices by JAX's collectives and lax.ppermute only.
A program may use at most 64 MiB of HBM per device.

v0:
```python
import jax
import jax.numpy as jnp
from jax import lax
from jax.sharding import PartitionSpec as P


def tile_terms(row_side, col_side, tile_blocks, pointers, columns):
    slot_ids = jnp.arange(tile_blocks.shape[0], dtype=jnp.int32)
    live_slots = slot_ids < pointers[-1]
    slot_rows = jnp.sum((slot_ids[:, None] >= pointers[None, 1:]).astype(jnp.int32), axis=1)
    slot_rows = jnp.minimum(slot_rows, pointers.shape[0] - 2)
    count_vectors = row_side.shape[0]
    edge = tile_blocks.shape[1]
    row_blocks = row_side.reshape(count_vectors, -1, edge)
    col_blocks = col_side.reshape(count_vectors, -1, edge)
    picked_rows = jnp.take(row_blocks, slot_rows, axis=1)
    picked_cols = jnp.take(col_blocks, columns, axis=1)
    forward = jnp.einsum(
        "ksj,sij->ski", picked_cols, tile_blocks, preferred_element_type=jnp.float32
    )
    backward = jnp.einsum(
        "ksi,sij->skj", picked_rows, tile_blocks, preferred_element_type=jnp.float32
    )
    live_mask = live_slots[:, None, None]
    forward = jnp.where(live_mask, forward, jnp.zeros_like(forward))
    backward = jnp.where(live_mask, backward, jnp.zeros_like(backward))
    forward_sum = jax.ops.segment_sum(
        forward, slot_rows, num_segments=row_blocks.shape[1], indices_are_sorted=True
    )
    backward_sum = jax.ops.segment_sum(backward, columns, num_segments=col_blocks.shape[1])
    return (forward_sum, backward_sum)


def body(vectors, blocks, row_ptr, col_idx):
    count_vectors = vectors.shape[0]
    segment = vectors.shape[1]
    grid_rows = lax.axis_size("row")
    grid_cols = lax.axis_size("col")
    everything = lax.all_gather(vectors, ("row", "col"), axis=1, tiled=True)
    row_side = lax.dynamic_slice_in_dim(
        everything, lax.axis_index("row") * (grid_cols * segment), grid_cols * segment, 1
    )
    spread = everything.reshape(count_vectors, grid_rows, grid_cols, segment)
    col_side = lax.dynamic_slice_in_dim(spread, lax.axis_index("col"), 1, 2).reshape(
        count_vectors, grid_rows * segment
    )
    forward_sum, backward_sum = tile_terms(row_side, col_side, blocks[0], row_ptr[0], col_idx[0])
    forward_part = lax.psum_scatter(forward_sum, "col", scatter_dimension=0, tiled=True)
    backward_part = lax.psum_scatter(backward_sum, "row", scatter_dimension=0, tiled=True)
    combined = forward_part + backward_part
    return combined.transpose(1, 0, 2).reshape(count_vectors, segment)


def solution(mesh):
    in_specs = (
        P(None, ("row", "col")),
        P("row", "col", None, None),
        P("row", "col"),
        P("row", "col"),
    )
    out_specs = P(None, ("row", "col"))
    return jax.shard_map(body, mesh=mesh, in_specs=in_specs, out_specs=out_specs, check_vma=False)
```

profile of v0, /device:TPU:8, one launch (start us, length us, event | category | flops | bytes accessed | tf_op | source)
XLA Modules:
  0.0 608.5 jit_solution(9309983485756426636)
XLA Ops:
  6.5 0.0 all-gather.2.cloned.1.call-start
  6.5 0.7 all-gather.2.cloned.1.call-update
  7.3 0.0 reduce-scatter.5.cloned.1.call-start
  7.3 1.2 slice.9
  8.5 0.6 iota_compare_fusion.1
  9.1 0.8 slice_bitcast_fusion
  9.9 0.1 convert_reduce_fusion
  10.1 0.7 compare_and_fusion.1
  10.7 0.7 compare_select_fusion.1
  11.4 413.9 %all-gather.2.cloned.1.call-done = bf16[16,131072]{1,0:T(8,128)(2,1)} async-done(((bf16[16,512]{1,0:T(8,128)(2,1)}), bf16[16,131072]{1,0:T(8,128)(2,1)}) %all-gather.2.cloned.1.call-update) | async-done | bytes 4194320 | tf_op jit(solution)/shard_map/all_gather | solution.py:39
  425.3 1.1 copy_bitcast_fusion
  426.4 0.8 gather_fusion.1
  427.2 0.0 copy-start.2
  427.2 4.2 fusion.7
  431.5 0.0 copy-done.2
  431.5 7.6 %scatter_fusion.1 = f32[32,16,128]{2,1,0:T(8,128)S(1)} fusion(f32[32,16,128]{2,1,0:T(8,128)S(1)} %broadcast_in_dim.43, s32[192]{0:T(256)S(1)} %bitcast.42, f32[192,16,128]{2,1,0:T(8,128)S(1)} %fusion.7), kind=kCustom, calls=%fused_computation.3 | custom fusion | flops 393216 | bytes 4719360 | tf_op jit(solution)/shard_map/scatter-add | solution.py:30
  439.1 0.0 copy-start
  439.1 0.7 copy-done
  439.8 0.0 reduce-scatter.5.cloned.1.call-update
  439.8 0.0 reduce-scatter.3.cloned.1.call-start
  439.9 3.6 copy.18
  443.5 0.8 dynamic-slice_reduce_fusion
  444.3 0.1 reshape_reshape.3
  444.4 0.1 copy.12
  444.4 0.8 gather_fusion
  445.2 5.8 fusion.4
  451.0 0.1 broadcast_in_dim.39
  451.1 7.9 %scatter_fusion = f32[128,16,128]{2,1,0:T(8,128)S(1)} fusion(f32[128,16,128]{2,1,0:T(8,128)S(1)} %broadcast_in_dim.39, s32[192]{0:T(256)S(1)} %broadcast_minimum_fusion, f32[192,16,128]{2,1,0:T(8,128)S(1)} %fusion.4), kind=kCustom, calls=%fused_computation.2 | custom fusion | flops 393216 | bytes 4719360 | tf_op jit(solution)/shard_map/scatter-add | solution.py:27
  459.1 0.0 copy-start.1
  459.1 1.0 copy-done.1
  460.1 0.0 reduce-scatter.3.cloned.1.call-update
  460.1 19.7 %reduce-scatter.5.cloned.1.call-done = f32[4,16,128]{2,1,0:T(8,128)} async-done(((f32[32,16,128]{2,1,0:T(8,128)}), f32[4,16,128]{2,1,0:T(8,128)}) %reduce-scatter.5.cloned.1.call-update) | async-done | bytes 32784 | tf_op jit(solution)/shard_map/reduce_scatter | solution.py:49
  479.8 120.8 %reduce-scatter.3.cloned.1.call-done = f32[4,16,128]{2,1,0:T(8,128)} async-done(((f32[128,16,128]{2,1,0:T(8,128)}), f32[4,16,128]{2,1,0:T(8,128)}) %reduce-scatter.3.cloned.1.call-update) | async-done | bytes 32784 | tf_op jit(solution)/shard_map/reduce_scatter | solution.py:48
  600.6 1.4 copy_bitcast_fusion.1
  (6 shorter events, 0.1 us)
Async XLA Ops:
  6.5 418.8 %all-gather.2.cloned.1.call-start = ((), (), s32[]{:S(2)}) async-start(), calls=%async_computation.2 | async-start | bytes 4210688 | tf_op jit(solution)/shard_map/all_gather | solution.py:39
  7.3 472.5 %reduce-scatter.5.cloned.1.call-start = ((), (), s32[]{:S(2)}) async-start(), calls=%async_computation.4 | async-start | bytes 294912 | tf_op jit(solution)/shard_map/reduce_scatter | solution.py:49
  427.2 4.3 copy-start.2
  439.1 0.7 copy-start
  439.8 160.8 %reduce-scatter.3.cloned.1.call-start = ((), (), s32[]{:S(2)}) async-start(), calls=%async_computation.3 | async-start | bytes 1081344 | tf_op jit(solution)/shard_map/reduce_scatter | solution.py:48
  459.1 1.0 copy-start.1
Sparse Core Ops, SparseCore 0:
  9.2 416.0 all-gather.1
  439.9 39.8 reduce-scatter.4
  483.9 116.6 reduce-scatter.2
where the time goes:
time: 609 us
  waiting for transfers between devices  555 us (91%)
  other arithmetic  19.1 us (3%)
  between operations  13.3 us (2%)
  local copies, waits for them, and re-layouts  10.9 us (2%)
  matrix products  10.1 us (2%)
    all_gather x1, waiting for transfers between devices, body(): everything = lax.all_gather(vectors, ('row', 'col'), axis=1, tiled=True)  414 us
    reduce_scatter x1, waiting for transfers between devices, body(): lax.psum_scatter(forward_sum, 'col', scatter_dimension=0, tiled=True)  121 us
    reduce_scatter x1, waiting for transfers between devices, body(): lax.psum_scatter(backward_sum, 'row', scatter_dimension=0, tiled=True)  19.7 us
  transfers between devices with their start and end apart: 3, of which 3 were waited for; matrix products, arithmetic and copies ran while one was open for 4% of the time, Pallas kernels for 0%

commit v1 on v0

--- a/solution.py
+++ b/solution.py
@@ -36,7 +36,10 @@
     segment = vectors.shape[1]
     grid_rows = lax.axis_size("row")
     grid_cols = lax.axis_size("col")
-    everything = lax.all_gather(vectors, ("row", "col"), axis=1, tiled=True)
+    everything = jnp.concatenate(
+        lax.all_to_all(jnp.stack([vectors] * lax.axis_size(("row", "col"))), ("row", "col"), 0, 0),
+        axis=1,
+    )
     row_side = lax.dynamic_slice_in_dim(
         everything, lax.axis_index("row") * (grid_cols * segment), grid_cols * segment, 1
     )

time: 609 us -> 301 us (0.49)
  waiting for transfers between devices: 555 us -> 233 us
  starting transfers between devices: 0.08 us -> 15.7 us
    all_gather x1 -> x0, waiting for transfers between devices: 414 us -> none  [body(): everything = lax.all_gather(vectors, ('row', 'col'), axis=1, tiled=True)]
    all_to_all x0 -> x1, waiting for transfers between devices: none -> 92.5 us  [body(): lax.all_to_all(jnp.stack([vectors] * lax.axis_size(('row', 'col'))), ('ro...]
    all_to_all x0 -> x1, starting transfers between devices: none -> 15.6 us  [body(): lax.all_to_all(jnp.stack([vectors] * lax.axis_size(('row', 'col'))), ('ro...]
  transfers between devices with their start and end apart: 3 -> 3, of which waited for: 3 -> 3; matrix products, arithmetic and copies ran while one was open for 4% -> 6% of each run, Pallas kernels for 0% -> 0%
where the time goes in v1:
time: 301 us
  waiting for transfers between devices  233 us (77%)
  other arithmetic  17.7 us (6%)
  starting transfers between devices  15.7 us (5%)
  between operations  13.6 us (5%)
  local copies, waits for them, and re-layouts  10.9 us (4%)
  matrix products  10.1 us (3%)
    reduce_scatter x1, waiting for transfers between devices, body(): lax.psum_scatter(forward_sum, 'col', scatter_dimension=0, tiled=True)  121 us
    all_to_all x1, waiting for transfers between devices, body(): lax.all_to_all(jnp.stack([vectors] * lax.axis_size(('row', 'col'))), ('ro...  92.5 us
    reduce_scatter x1, waiting for transfers between devices, body(): lax.psum_scatter(backward_sum, 'row', scatter_dimension=0, tiled=True)  19.3 us
    all_to_all x1, starting transfers between devices, body(): lax.all_to_all(jnp.stack([vectors] * lax.axis_size(('row', 'col'))), ('ro...  15.6 us
    scatter-add x1, other arithmetic, tile_terms(): jax.ops.segment_sum(forward, slot_rows, num_segments=row_blocks.shape[1],...  7.95 us
    scatter-add x1, other arithmetic, tile_terms(): jax.ops.segment_sum(backward, columns, num_segments=col_blocks.shape[1])  7.57 us
  transfers between devices with their start and end apart: 3, of which 3 were waited for; matrix products, arithmetic and copies ran while one was open for 6% of the time, Pallas kernels for 0%

profile of v1, /device:TPU:8, one launch (start us, length us, event | category | flops | bytes accessed | tf_op | source)
XLA Modules:
  0.0 300.6 jit_solution(6476918184411494468)
XLA Ops:
  6.5 3.2 %stack.2 = bf16[256,16,512]{2,1,0:T(8,128)(2,1)} broadcast(bf16[16,512]{1,0:T(8,128)(2,1)} %param.4), dimensions={1,2} | broadcast | bytes 4210688 | tf_op jit(solution)/shard_map/stack | solution.py:40
  9.8 0.0 copy-start.3
  9.8 0.0 copy-start.2
  9.8 15.6 %all-to-all-start = ((bf16[256,16,512]{2,1,0:T(8,128)(2,1)}), bf16[256,16,512]{2,1,0:T(8,128)(2,1)}, u32[]{:S(2)}, u32[]{:S(2)}) async-start(bf16[256,16,512]{2,1,0:T(8,128)(2,1)} %stack.2), calls=%async_computation | async-start | bytes 8388608 | tf_op jit(solution)/shard_map/all_to_all | solution.py:40
  25.4 0.0 reduce-scatter.5.cloned.1.call-start
  25.4 0.0 copy-done.3
  25.4 0.5 slice.9
  25.9 0.6 iota_compare_fusion.1
  26.6 0.1 slice_bitcast_fusion
  26.7 0.1 convert_reduce_fusion
  26.8 0.0 copy-done.2
  26.9 92.5 %all-to-all-done = bf16[256,16,512]{2,1,0:T(8,128)(2,1)} async-done(((bf16[256,16,512]{2,1,0:T(8,128)(2,1)}), bf16[256,16,512]{2,1,0:T(8,128)(2,1)}, u32[]{:S(2)}, u32[]{:S(2)}) %all-to-all-start) | async-done | bytes 4194336 | tf_op jit(solution)/shard_map/all_to_all | solution.py:40
  119.4 2.5 copy.23
  121.9 0.1 copy_bitcast_fusion
  122.0 0.8 gather_fusion.1
  122.8 4.2 %fusion.7 = f32[192,16,128]{2,1,0:T(8,128)S(1)} fusion(bf16[1,192,128,128]{3,2,1,0:T(8,128)(2,1)} %param.5, bf16[192,16,128]{2,1,0:T(8,128)(2,1)S(1)} %gather_fusion.1, pred[192]{0:T(512)(128)(4,1)S(1)} %compare_and_fusion, pred[192]{0:T(512)(128)(4,1)S(1)} %iota_compare_fusion.1), kind=kOutput, calls=%fused_computation.9 | convolution fusion | flops 101449728 | bytes 8651136 | tf_op jit(solution)/shard_map/ksi,sij->skj/dot_general | solution.py:21
  127.1 7.6 %scatter_fusion.1 = f32[32,16,128]{2,1,0:T(8,128)S(1)} fusion(f32[32,16,128]{2,1,0:T(8,128)S(1)} %broadcast_in_dim.43, s32[192]{0:T(256)S(1)} %bitcast.47, f32[192,16,128]{2,1,0:T(8,128)S(1)} %fusion.7), kind=kCustom, calls=%fused_computation.3 | custom fusion | flops 393216 | bytes 4719360 | tf_op jit(solution)/shard_map/scatter-add | solution.py:30
  134.6 0.0 copy-start
  134.7 0.7 copy-done
  135.3 0.0 reduce-scatter.5.cloned.1.call-update
  135.4 0.0 reduce-scatter.3.cloned.1.call-start
  135.4 0.9 constant_dynamic-slice_fusion
  136.3 0.1 copy.21
  136.4 0.1 reshape_reshape.7
  136.5 0.1 copy.17
  136.6 0.8 gather_fusion
  137.4 5.8 %fusion.4 = f32[192,16,128]{2,1,0:T(8,128)S(1)} fusion(bf16[1,192,128,128]{3,2,1,0:T(8,128)(2,1)} %param.5, bf16[192,16,128]{2,1,0:T(8,128)(2,1)S(1)} %gather_fusion, pred[192]{0:T(512)(128)(4,1)S(1)} %compare_and_fusion.1, pred[192]{0:T(512)(128)(4,1)S(1)} %iota_compare_fusion.1), kind=kOutput, calls=%fused_computation.8 | convolution fusion | flops 101449728 | bytes 8651136 | tf_op jit(solution)/shard_map/ksj,sij->ski/dot_general | solution.py:18
  143.2 0.1 broadcast_in_dim.39
  143.3 7.9 %scatter_fusion = f32[128,16,128]{2,1,0:T(8,128)S(1)} fusion(f32[128,16,128]{2,1,0:T(8,128)S(1)} %broadcast_in_dim.39, s32[192]{0:T(256)S(1)} %broadcast_minimum_fusion, f32[192,16,128]{2,1,0:T(8,128)S(1)} %fusion.4), kind=kCustom, calls=%fused_computation.2 | custom fusion | flops 393216 | bytes 4719360 | tf_op jit(solution)/shard_map/scatter-add | solution.py:27
  151.2 0.0 copy-start.1
  151.2 1.0 copy-done.1
  152.2 0.0 reduce-scatter.3.cloned.1.call-update
  152.2 19.3 %reduce-scatter.5.cloned.1.call-done = f32[4,16,128]{2,1,0:T(8,128)} async-done(((f32[32,16,128]{2,1,0:T(8,128)}), f32[4,16,128]{2,1,0:T(8,128)}) %reduce-scatter.5.cloned.1.call-update) | async-done | bytes 32784 | tf_op jit(solution)/shard_map/reduce_scatter | solution.py:52
  171.5 120.8 %reduce-scatter.3.cloned.1.call-done = f32[4,16,128]{2,1,0:T(8,128)} async-done(((f32[128,16,128]{2,1,0:T(8,128)}), f32[4,16,128]{2,1,0:T(8,128)}) %reduce-scatter.3.cloned.1.call-update) | async-done | bytes 32784 | tf_op jit(solution)/shard_map/reduce_scatter | solution.py:51
  292.3 1.4 copy_bitcast_fusion.1
  (8 shorter events, 0.1 us)
Async XLA Ops:
  9.8 15.7 %copy-start.3 = (s32[1,129]{1,0:T(1,128)S(1)}, s32[1,129]{1,0:T(1,128)}, u32[]{:S(2)}) copy-start(s32[1,129]{1,0:T(1,128)} %param.6) | copy-start | bytes 1552
  9.8 17.1 %copy-start.2 = (s32[1,192]{1,0:T(1,128)S(1)}, s32[1,192]{1,0:T(1,128)}, u32[]{:S(2)}) copy-start(s32[1,192]{1,0:T(1,128)} %param.7) | copy-start | bytes 2308
  9.8 109.6 %all-to-all-start = ((bf16[256,16,512]{2,1,0:T(8,128)(2,1)}), bf16[256,16,512]{2,1,0:T(8,128)(2,1)}, u32[]{:S(2)}, u32[]{:S(2)}) async-start(bf16[256,16,512]{2,1,0:T(8,128)(2,1)} %stack.2), calls=%async_computation | async-start | bytes 8388608 | tf_op jit(solution)/shard_map/all_to_all | solution.py:40
  25.4 146.1 %reduce-scatter.5.cloned.1.call-start = ((), (), s32[]{:S(2)}) async-start(), calls=%async_computation.4 | async-start | bytes 294912 | tf_op jit(solution)/shard_map/reduce_scatter | solution.py:52
  134.6 0.7 copy-start
  135.4 157.0 %reduce-scatter.3.cloned.1.call-start = ((), (), s32[]{:S(2)}) async-start(), calls=%async_computation.3 | async-start | bytes 1081344 | tf_op jit(solution)/shard_map/reduce_scatter | solution.py:51
  151.2 1.0 copy-start.1
Sparse Core Ops, SparseCore 0:
  135.5 35.9 reduce-scatter.4
  175.6 116.7 reduce-scatter.2
